TPU v7x, 512 devices: a whole 4x4x16 slice. The times are simulated.
512 devices in a mesh: gx: 32 (over z_hi, x, core), gy: 16 (over y, z_lo).
Axes of the slice: x: 4, y: 4, z: 16 (z_hi: 4, z_lo: 4; z = z_hi * 4 + z_lo), core: 2. Of those that a mesh axis runs over, the one named last changes fastest.
Arguments:
- orbitals: float32 [32, 64, 128, 512], P(None, 'gx', 'gy'), may hold values from -60 to 60
- potential: float32 [64, 128, 512], P('gx', 'gy'), may hold values from 0.2 to 2
- sign_bits: int32 [64, 128, 512], P('gx', 'gy'), may hold values from 0 to 1
- sampled_rows: int32 [32, 16, 8192], P('gx', 'gy'), may hold values from 0 to 8191, each once within a row
Outputs:
- rotated: float32 [32, 64, 128, 512], P(None, 'gx', 'gy')
- sketches: float32 [2, 32, 4096], P(None, None, ('gx', 'gy'))
- projected: float32 [32, 32], replicated
Inputs may be any that keep to these rules, and one draw needn't show every extreme that they name: Each block's row of sampled_rows holds every one of its 8192 cell numbers once.
All inputs are finite; a program needn't handle non-finite values.
Results may differ from a plain program's by a relative error of at most 0.00026.
Values sent between devices are 32-bit elements; how exact they have to be, the bound alone decides.
No kernel may reach another device: no remote copies, remote signals or barrier semaphores. Data moves between devices by JAX's collectives and lax.ppermute only.
A program may use at most 64 MiB of HBM per device.

v0:
```python
import jax
import jax.numpy as jnp
from jax import lax
from jax.sharding import PartitionSpec as P

M = 4096
HIGHEST = lax.Precision.HIGHEST
filter_center = 6.25
filter_half = 4.25


def padded_2(array, sides, width):
    for axis, dim in sides:
        size, length = (lax.axis_size(axis), array.shape[dim])
        up = [(i, (i + 1) % size) for i in range(size - 1)]
        down = [(j, i) for i, j in up]
        last = lax.slice_in_dim(array, length - width, length, axis=dim)
        initial = lax.slice_in_dim(array, 0, width, axis=dim)
        before = lax.ppermute(last, axis, up)
        after = lax.ppermute(initial, axis, down)
        array = jnp.concatenate([before, array, after], axis=dim)
    return array


def hadamard_table(order):
    index = jnp.arange(order, dtype=jnp.int32)
    parity = jnp.zeros((order, order), jnp.int32)
    for bit in range(order.bit_length() - 1):
        weight = 2**bit
        parity = parity + index[:, None] // weight % 2 * (index[None, :] // weight % 2)
    return (1 - 2 * (parity % 2)).astype(jnp.float32)


def second_diff(padded, axis, count):
    parts = [lax.slice_in_dim(padded, k, k + count, axis=axis) for k in range(5)]
    return (16.0 * (parts[1] + parts[3]) - (parts[0] + parts[4]) - 30.0 * parts[2]) / 12.0


def apply_ham(field, potential):
    padded = padded_2(field, (("gx", 1), ("gy", 2)), 2)
    x_padded = padded[:, :, 2:-2, :]
    y_padded = padded[:, 2:-2, :, :]
    z_padded = jnp.pad(field, ((0, 0), (0, 0), (0, 0), (2, 2)))
    total = second_diff(x_padded, 1, field.shape[1])
    total = total + second_diff(y_padded, 2, field.shape[2])
    total = total + second_diff(z_padded, 3, field.shape[3])
    return -0.5 * total + potential[None] * field


def shards(orbitals, potential, sign_bits, sampled_rows):
    first = (apply_ham(orbitals, potential) - filter_center * orbitals) / filter_half
    second = 2.0 * (apply_ham(first, potential) - filter_center * first) / filter_half - orbitals
    filtered = 2.0 * (apply_ham(second, potential) - filter_center * second) / filter_half - first
    applied = apply_ham(filtered, potential)
    count = orbitals.shape[0]
    cells = orbitals.shape[1] * orbitals.shape[2] * orbitals.shape[3]
    stacked = jnp.concatenate([filtered, applied], axis=0)
    sign_block = (2 * sign_bits - 1).astype(jnp.float32)
    flat = (stacked * sign_block[None]).reshape(2 * count, -1, 128)
    mixed = jnp.einsum("nac,cd->nad", flat, hadamard_table(128), precision=HIGHEST)
    mixed = jnp.einsum("ba,nac->nbc", hadamard_table(cells // 128), mixed, precision=HIGHEST)
    mixed = mixed.reshape(2 * count, cells)
    picked = jnp.take(mixed, sampled_rows[0, 0, :M], axis=1)
    devices = lax.axis_size("gx") * lax.axis_size("gy")
    term = (picked / jnp.sqrt(jnp.float32(M * devices))).reshape(2, count, M)
    width = M // devices
    total = lax.psum(term, ("gx", "gy"))
    position = lax.axis_index("gx") * lax.axis_size("gy") + lax.axis_index("gy")
    share = lax.dynamic_slice_in_dim(total, position * width, width, 2)
    gram = jnp.dot(total[0], total[0].T, precision=HIGHEST) / cells
    cross = jnp.dot(total[0], total[1].T, precision=HIGHEST) / cells
    lower = jnp.linalg.cholesky(gram)
    inverse = lax.linalg.triangular_solve(
        lower, jnp.eye(count, dtype=jnp.float32), left_side=True, lower=True
    )
    rotated = jnp.dot(inverse, filtered.reshape(count, -1), precision=HIGHEST).reshape(
        filtered.shape
    )
    inner = jnp.dot(jnp.dot(inverse, cross, precision=HIGHEST), inverse.T, precision=HIGHEST)
    projected = 0.5 * (inner + inner.T)
    return (rotated, share, projected)


def solution(mesh):
    in_specs = (
        P(None, "gx", "gy", None),
        P("gx", "gy", None),
        P("gx", "gy", None),
        P("gx", "gy", None),
    )
    out_specs = (P(None, "gx", "gy", None), P(None, None, ("gx", "gy")), P())
    return jax.shard_map(shards, mesh=mesh, in_specs=in_specs, out_specs=out_specs, check_vma=False)
```

profile of v0, /device:TPU:1, one launch (start us, length us, event | category | flops | bytes accessed | tf_op | source)
XLA Modules:
  0.0 938.2 jit_solution(11268816920238034277)
XLA Ops:
  7.2 1.9 copy.36
  9.1 4.5 collective-permute-start
  13.7 5.6 collective-permute-start.1
  19.3 6.1 collective-permute-done
  25.5 0.6 constant_dynamic-update-slice_fusion.1
  26.1 4.0 collective-permute-done.1
  30.2 0.1 fusion.159
  30.3 3.6 collective-permute-start.2
  33.9 1.3 collective-permute-start.3
  35.2 7.6 collective-permute-done.2
  42.8 28.2 %collective-permute-done.3 = f32[32,6,2,512]{3,0,2,1:T(8,128)S(1)} collective-permute-done((f32[32,6,2,512]{3,0,2,1:T(8,128)S(1)}, f32[32,6,2,512]{3,0,2,1:T(8,128)S(1)}, u32[]{:S(2)}, u32[]{:S(2)}) %collective-permute-start.3) | collective-permute-done | bytes 786464 | tf_op jit(solution)/shard_map/ppermute | solution.py:20
  71.0 1.6 broadcast_multiply_fusion
  72.6 2.7 collective-permute-start.4
  75.3 1.9 collective-permute-start.5
  77.3 9.8 %collective-permute-done.4 = f32[32,2,8,512]{3,0,2,1:T(8,128)S(1)} collective-permute-done((f32[32,2,8,512]{3,0,2,1:T(8,128)S(1)}, f32[32,2,8,512]{3,0,2,1:T(8,128)S(1)}, u32[]{:S(2)}, u32[]{:S(2)}) %collective-permute-start.4) | collective-permute-done | bytes 1048608 | tf_op jit(solution)/shard_map/ppermute | solution.py:19
  87.1 4.4 collective-permute-done.5
  91.6 7.8 collective-permute-start.6
  99.4 1.3 collective-permute-start.7
  100.7 7.6 collective-permute-done.6
  108.2 26.3 %collective-permute-done.7 = f32[32,6,2,512]{3,0,2,1:T(8,128)S(1)} collective-permute-done((f32[32,6,2,512]{3,0,2,1:T(8,128)S(1)}, f32[32,6,2,512]{3,0,2,1:T(8,128)S(1)}, u32[]{:S(2)}, u32[]{:S(2)}) %collective-permute-start.7) | collective-permute-done | bytes 786464 | tf_op jit(solution)/shard_map/ppermute | solution.py:20
  134.6 2.4 fusion.21
  136.9 1.9 collective-permute-start.8
  138.9 2.5 collective-permute-start.9
  141.3 9.2 collective-permute-done.8
  150.6 4.4 collective-permute-done.9
  155.1 3.0 collective-permute-start.10
  158.2 1.3 collective-permute-start.11
  159.5 7.5 collective-permute-done.10
  167.0 24.4 %collective-permute-done.11 = f32[32,6,2,512]{3,0,2,1:T(8,128)S(1)} collective-permute-done((f32[32,6,2,512]{3,0,2,1:T(8,128)S(1)}, f32[32,6,2,512]{3,0,2,1:T(8,128)S(1)}, u32[]{:S(2)}, u32[]{:S(2)}) %collective-permute-start.11) | collective-permute-done | bytes 786464 | tf_op jit(solution)/shard_map/ppermute | solution.py:20
  191.4 1.8 fusion.32
  193.2 1.9 collective-permute-start.12
  195.1 2.5 collective-permute-start.13
  197.7 9.1 collective-permute-done.12
  206.8 22.0 %collective-permute-done.13 = f32[32,2,8,512]{3,0,2,1:T(8,128)S(1)} collective-permute-done((f32[32,2,8,512]{3,0,2,1:T(8,128)S(1)}, f32[32,2,8,512]{3,0,2,1:T(8,128)S(1)}, u32[]{:S(2)}, u32[]{:S(2)}) %collective-permute-start.13) | collective-permute-done | bytes 1048608 | tf_op jit(solution)/shard_map/ppermute | solution.py:20
  228.8 1.5 pad_maximum_fusion.30
  230.3 3.5 collective-permute-start.14
  233.7 1.3 collective-permute-start.15
  235.1 0.6 copy.46
  235.7 6.3 collective-permute-done.14
  242.1 27.8 %collective-permute-done.15 = f32[32,6,2,512]{3,0,2,1:T(8,128)} collective-permute-done((f32[32,6,2,512]{3,0,2,1:T(8,128)}, f32[32,6,2,512]{3,0,2,1:T(8,128)}, u32[]{:S(2)}, u32[]{:S(2)}) %collective-permute-start.15) | collective-permute-done | bytes 786464 | tf_op jit(solution)/shard_map/ppermute | solution.py:20
  269.9 3.4 fusion.40
  273.2 1.6 copy.47
  274.8 1.3 concatenate.101
  276.1 2.0 fusion
  278.1 2.1 convolution_bitcast_fusion
  280.2 2.7 copy.57
  282.9 13.0 %gather_fusion = f32[4096,64]{1,0:T(8,128)S(1)} fusion(f32[64,8192]{0,1:T(8,128)} %bitcast.60, s32[4096]{0:T(1024)S(1)} %broadcast_clamp_fusion), kind=kCustom, calls=%fused_computation | custom fusion | bytes 2113536 | tf_op jit(solution)/shard_map/jit(_take)/gather | solution.py:63
  295.9 1.6 copy.49
  297.5 2.3 select_multiply_fusion
  299.8 0.6 copy.59
  300.4 614.8 %all-reduce.6.cloned.1.call-done = f32[2,32,4096]{2,1,0:T(8,128)} async-done(((f32[2,32,4096]{2,1,0:T(8,128)}), f32[2,32,4096]{2,1,0:T(8,128)}) %all-reduce.6.cloned.1.call-update) | async-done | bytes 1048592 | tf_op jit(solution)/shard_map/psum | solution.py:67
  915.2 1.8 fusion.81
  917.0 2.9 cholesky.17
  920.0 0.6 compare_reduce_fusion
  920.6 0.7 fusion.117
  921.3 2.4 custom-call.6
  923.7 0.2 fusion.120
  923.9 1.8 convolution_multiply_fusion
  925.9 0.2 fusion.161
  926.1 0.6 fusion.119
  926.7 1.6 fusion.78
  928.3 1.6 copy.54
  929.9 0.8 constant_dynamic-slice_fusion
  930.7 0.7 copy.55
  (39 shorter events, 1.0 us)
Async XLA Ops:
  7.2 18.3 %copy-start = (f32[32,2,8,512]{3,2,1,0:T(8,128)S(1)}, f32[32,2,8,512]{3,2,1,0:T(8,128)}, u32[]{:S(2)}) copy-start(f32[32,2,8,512]{3,2,1,0:T(8,128)} %param.4) | copy-start | bytes 3145732
  7.2 908.0 %all-reduce.6.cloned.1.call-start = ((), (), s32[]{:S(2)}) async-start(), calls=%async_computation | async-start | bytes 2097152 | tf_op jit(solution)/shard_map/psum | solution.py:67
  9.1 16.2 %collective-permute-start = (f32[32,2,8,512]{3,0,2,1:T(8,128)S(1)}, f32[32,2,8,512]{3,0,2,1:T(8,128)S(1)}, u32[]{:S(2)}, u32[]{:S(2)}) collective-permute-start(f32[32,2,8,512]{3,0,2,1:T(8,128)S(1)} %copy.36), channel_id=1, source_target_pairs={{0,16},{16,32},{32,48},{48,64},{64,80},{80,96},{96,112},{112,128},... | collective-permute-start | bytes 3145736 | tf_op jit(solution)/shard_map/ppermute | solution.py:19
  13.7 16.4 %collective-permute-start.1 = (f32[32,2,8,512]{3,0,2,1:T(8,128)S(1)}, f32[32,2,8,512]{3,0,2,1:T(8,128)S(1)}, u32[]{:S(2)}, u32[]{:S(2)}) collective-permute-start(f32[32,2,8,512]{3,0,2,1:T(8,128)S(1)} %copy.36), channel_id=1, source_target_pairs={{16,0},{32,16},{48,32},{64,48},{80,64},{96,80},{112,96},{128,112},... | collective-permute-start | bytes 3145736 | tf_op jit(solution)/shard_map/ppermute | solution.py:20
  30.2 40.8 %copy-start.3 = (f32[2,8,512]{2,1,0:T(8,128)S(1)}, f32[2,8,512]{2,1,0:T(8,128)}, u32[]{:S(2)}) copy-start(f32[2,8,512]{2,1,0:T(8,128)} %param.5) | copy-start | bytes 98308
  30.3 12.5 %collective-permute-start.2 = (f32[32,6,2,512]{3,0,2,1:T(8,128)S(1)}, f32[32,6,2,512]{3,0,2,1:T(8,128)S(1)}, u32[]{:S(2)}, u32[]{:S(2)}) collective-permute-start(f32[32,6,2,512]{3,0,2,1:T(8,128)S(1)} %get-tuple-element.23), channel_id=1, source_target_pairs={{0,1},{1,2},{2,3},{3,4},{4,5},{5,6},{6,7},{7,8},{8,9},{9,10},{10,1... | collective-permute-start | bytes 2359304 | tf_op jit(solution)/shard_map/ppermute | solution.py:19
  33.9 37.1 %collective-permute-start.3 = (f32[32,6,2,512]{3,0,2,1:T(8,128)S(1)}, f32[32,6,2,512]{3,0,2,1:T(8,128)S(1)}, u32[]{:S(2)}, u32[]{:S(2)}) collective-permute-start(f32[32,6,2,512]{3,0,2,1:T(8,128)S(1)} %get-tuple-element.24), channel_id=1, source_target_pairs={{1,0},{2,1},{3,2},{4,3},{5,4},{6,5},{7,6},{8,7},{9,8},{10,9},{11,1... | collective-permute-start | bytes 2359304 | tf_op jit(solution)/shard_map/ppermute | solution.py:20
  72.6 14.4 %collective-permute-start.4 = (f32[32,2,8,512]{3,0,2,1:T(8,128)S(1)}, f32[32,2,8,512]{3,0,2,1:T(8,128)S(1)}, u32[]{:S(2)}, u32[]{:S(2)}) collective-permute-start(f32[32,2,8,512]{3,0,2,1:T(8,128)S(1)} %get-tuple-element.15), channel_id=1, source_target_pairs={{0,16},{16,32},{32,48},{48,64},{64,80},{80,96},{96,112},{112,128},... | collective-permute-start | bytes 3145736 | tf_op jit(solution)/shard_map/ppermute | solution.py:19
  75.3 16.1 %collective-permute-start.5 = (f32[32,2,8,512]{3,0,2,1:T(8,128)S(1)}, f32[32,2,8,512]{3,0,2,1:T(8,128)S(1)}, u32[]{:S(2)}, u32[]{:S(2)}) collective-permute-start(f32[32,2,8,512]{3,0,2,1:T(8,128)S(1)} %get-tuple-element.15), channel_id=1, source_target_pairs={{16,0},{32,16},{48,32},{64,48},{80,64},{96,80},{112,96},{128,112},... | collective-permute-start | bytes 3145736 | tf_op jit(solution)/shard_map/ppermute | solution.py:20
  91.6 16.7 %collective-permute-start.6 = (f32[32,6,2,512]{3,0,2,1:T(8,128)S(1)}, f32[32,6,2,512]{3,0,2,1:T(8,128)S(1)}, u32[]{:S(2)}, u32[]{:S(2)}) collective-permute-start(f32[32,6,2,512]{3,0,2,1:T(8,128)S(1)} %get-tuple-element.21), channel_id=1, source_target_pairs={{0,1},{1,2},{2,3},{3,4},{4,5},{5,6},{6,7},{7,8},{8,9},{9,10},{10,1... | collective-permute-start | bytes 2359304 | tf_op jit(solution)/shard_map/ppermute | solution.py:19
  99.4 35.2 %collective-permute-start.7 = (f32[32,6,2,512]{3,0,2,1:T(8,128)S(1)}, f32[32,6,2,512]{3,0,2,1:T(8,128)S(1)}, u32[]{:S(2)}, u32[]{:S(2)}) collective-permute-start(f32[32,6,2,512]{3,0,2,1:T(8,128)S(1)} %get-tuple-element.22), channel_id=1, source_target_pairs={{1,0},{2,1},{3,2},{4,3},{5,4},{6,5},{7,6},{8,7},{9,8},{10,9},{11,1... | collective-permute-start | bytes 2359304 | tf_op jit(solution)/shard_map/ppermute | solution.py:20
  136.9 13.7 %collective-permute-start.8 = (f32[32,2,8,512]{3,0,2,1:T(8,128)S(1)}, f32[32,2,8,512]{3,0,2,1:T(8,128)S(1)}, u32[]{:S(2)}, u32[]{:S(2)}) collective-permute-start(f32[32,2,8,512]{3,0,2,1:T(8,128)S(1)} %fusion.21), channel_id=1, source_target_pairs={{0,16},{16,32},{32,48},{48,64},{64,80},{80,96},{96,112},{112,128},... | collective-permute-start | bytes 3145736 | tf_op jit(solution)/shard_map/ppermute | solution.py:19
  138.9 16.1 %collective-permute-start.9 = (f32[32,2,8,512]{3,0,2,1:T(8,128)S(1)}, f32[32,2,8,512]{3,0,2,1:T(8,128)S(1)}, u32[]{:S(2)}, u32[]{:S(2)}) collective-permute-start(f32[32,2,8,512]{3,0,2,1:T(8,128)S(1)} %fusion.21), channel_id=1, source_target_pairs={{16,0},{32,16},{48,32},{64,48},{80,64},{96,80},{112,96},{128,112},... | collective-permute-start | bytes 3145736 | tf_op jit(solution)/shard_map/ppermute | solution.py:20
  155.1 11.9 %collective-permute-start.10 = (f32[32,6,2,512]{3,0,2,1:T(8,128)S(1)}, f32[32,6,2,512]{3,0,2,1:T(8,128)S(1)}, u32[]{:S(2)}, u32[]{:S(2)}) collective-permute-start(f32[32,6,2,512]{3,0,2,1:T(8,128)S(1)} %get-tuple-element.19), channel_id=1, source_target_pairs={{0,1},{1,2},{2,3},{3,4},{4,5},{5,6},{6,7},{7,8},{8,9},{9,10},{10,1... | collective-permute-start | bytes 2359304 | tf_op jit(solution)/shard_map/ppermute | solution.py:19
  158.1 39.4 %copy-start.5 = (s32[2,8,512]{2,1,0:T(8,128)S(1)}, s32[2,8,512]{2,1,0:T(8,128)}, u32[]{:S(2)}) copy-start(s32[2,8,512]{2,1,0:T(8,128)} %param.6) | copy-start | bytes 98308
  158.2 39.5 %slice-start = ((s32[1,1,8192]{2,1,0:T(1,128)}), s32[1,1,4096]{2,1,0:T(1,128)S(1)}, s32[]{:S(2)}) async-start(s32[1,1,8192]{2,1,0:T(1,128)} %param.7), calls=%async_computation.1 | async-start | bytes 32768 | tf_op jit(solution)/shard_map/slice | solution.py:63
  158.2 33.2 %collective-permute-start.11 = (f32[32,6,2,512]{3,0,2,1:T(8,128)S(1)}, f32[32,6,2,512]{3,0,2,1:T(8,128)S(1)}, u32[]{:S(2)}, u32[]{:S(2)}) collective-permute-start(f32[32,6,2,512]{3,0,2,1:T(8,128)S(1)} %get-tuple-element.20), channel_id=1, source_target_pairs={{1,0},{2,1},{3,2},{4,3},{5,4},{6,5},{7,6},{8,7},{9,8},{10,9},{11,1... | collective-permute-start | bytes 2359304 | tf_op jit(solution)/shard_map/ppermute | solution.py:20
  193.2 13.7 %collective-permute-start.12 = (f32[32,2,8,512]{3,0,2,1:T(8,128)S(1)}, f32[32,2,8,512]{3,0,2,1:T(8,128)S(1)}, u32[]{:S(2)}, u32[]{:S(2)}) collective-permute-start(f32[32,2,8,512]{3,0,2,1:T(8,128)S(1)} %fusion.32), channel_id=1, source_target_pairs={{0,16},{16,32},{32,48},{48,64},{64,80},{80,96},{96,112},{112,128},... | collective-permute-start | bytes 3145736 | tf_op jit(solution)/shard_map/ppermute | solution.py:19
  195.1 33.7 %collective-permute-start.13 = (f32[32,2,8,512]{3,0,2,1:T(8,128)S(1)}, f32[32,2,8,512]{3,0,2,1:T(8,128)S(1)}, u32[]{:S(2)}, u32[]{:S(2)}) collective-permute-start(f32[32,2,8,512]{3,0,2,1:T(8,128)S(1)} %fusion.32), channel_id=1, source_target_pairs={{16,0},{32,16},{48,32},{64,48},{80,64},{96,80},{112,96},{128,112},... | collective-permute-start | bytes 3145736 | tf_op jit(solution)/shard_map/ppermute | solution.py:20
  197.7 37.3 %copy-start.4 = (s32[1,1,8192]{2,1,0:T(1,128)S(1)}, s32[1,1,8192]{2,1,0:T(1,128)}, u32[]{:S(2)}) copy-start(s32[1,1,8192]{2,1,0:T(1,128)} %param.7) | copy-start | bytes 98308
  206.8 23.4 %copy-start.1 = (f32[32,2,8,512]{3,0,2,1:T(8,128)}, f32[32,2,8,512]{3,0,2,1:T(8,128)S(1)}, u32[]{:S(2)}) copy-start(f32[32,2,8,512]{3,0,2,1:T(8,128)S(1)} %collective-permute-done.12) | copy-start | bytes 3145732
  228.8 1.5 copy-start.2
  230.3 11.8 %collective-permute-start.14 = (f32[32,6,2,512]{3,0,2,1:T(8,128)}, f32[32,6,2,512]{3,0,2,1:T(8,128)}, u32[]{:S(2)}, u32[]{:S(2)}) collective-permute-start(f32[32,6,2,512]{3,0,2,1:T(8,128)} %get-tuple-element.17), channel_id=1, source_target_pairs={{0,1},{1,2},{2,3},{3,4},{4,5},{5,6},{6,7},{7,8},{8,9},{9,10},{10,1... | collective-permute-start | bytes 2359304 | tf_op jit(solution)/shard_map/ppermute | solution.py:19
  233.7 36.1 %collective-permute-start.15 = (f32[32,6,2,512]{3,0,2,1:T(8,128)}, f32[32,6,2,512]{3,0,2,1:T(8,128)}, u32[]{:S(2)}, u32[]{:S(2)}) collective-permute-start(f32[32,6,2,512]{3,0,2,1:T(8,128)} %get-tuple-element.18), channel_id=1, source_target_pairs={{1,0},{2,1},{3,2},{4,3},{5,4},{6,5},{7,6},{8,7},{9,8},{10,9},{11,1... | collective-permute-start | bytes 2359304 | tf_op jit(solution)/shard_map/ppermute | solution.py:20
Sparse Core Ops, SparseCore 0:
  299.9 615.2 all-reduce.5
where the time goes:
time: 939 us; the launch traced here: 938 us
  waiting for transfers between devices  819 us (87%)
  starting transfers between devices  46.6 us (5%)
  local copies, waits for them, and re-layouts  27.6 us (3%)
  other arithmetic  20.5 us (2%)
  between operations  14.5 us (2%)
  matrix products  9.67 us (1%)
    psum x1, waiting for transfers between devices, shards(): total = lax.psum(term, ('gx', 'gy'))  615 us
    ppermute x8, waiting for transfers between devices, padded_2(): after = lax.ppermute(initial, axis, down)  141 us
    ppermute x8, waiting for transfers between devices, padded_2(): before = lax.ppermute(last, axis, up)  63.2 us
    ppermute x8, starting transfers between devices, padded_2(): before = lax.ppermute(last, axis, up)  28.9 us
  transfers between devices with their start and end apart: 17, of which 17 were waited for; matrix products, arithmetic and copies ran while one was open for 0% of the time, Pallas kernels for 0%

commit v1 on v0

--- a/solution.py
+++ b/solution.py
@@ -64,7 +64,7 @@
     devices = lax.axis_size("gx") * lax.axis_size("gy")
     term = (picked / jnp.sqrt(jnp.float32(M * devices))).reshape(2, count, M)
     width = M // devices
-    total = lax.psum(term, ("gx", "gy"))
+    total = lax.psum(lax.psum(term, "gx"), "gy")
     position = lax.axis_index("gx") * lax.axis_size("gy") + lax.axis_index("gy")
     share = lax.dynamic_slice_in_dim(total, position * width, width, 2)
     gram = jnp.dot(total[0], total[0].T, precision=HIGHEST) / cells

time: 939 us -> 1000 us (1.065)
  waiting for transfers between devices: 819 us -> 872 us
    psum x1 -> x2, waiting for transfers between devices: 615 us -> 668 us  [shards(): total = lax.psum(lax.psum(term, 'gx'), 'gy')]
  transfers between devices with their start and end apart: 17 -> 18, of which waited for: 17 -> 18; matrix products, arithmetic and copies ran while one was open for 0% -> 0% of each run, Pallas kernels for 0% -> 0%
where the time goes in v1:
time: 1000 us; the launch traced here: 991 us
  waiting for transfers between devices  872 us (87%)
  starting transfers between devices  47 us (5%)
  local copies, waits for them, and re-layouts  27.6 us (3%)
  other arithmetic  20.3 us (2%)
  between operations  14.5 us (1%)
    psum x2, waiting for transfers between devices, shards(): total = lax.psum(lax.psum(term, 'gx'), 'gy')  668 us
    ppermute x8, waiting for transfers between devices, padded_2(): after = lax.ppermute(initial, axis, down)  141 us
    ppermute x8, waiting for transfers between devices, padded_2(): before = lax.ppermute(last, axis, up)  63 us
    ppermute x8, starting transfers between devices, padded_2(): before = lax.ppermute(last, axis, up)  28.9 us
  transfers between devices with their start and end apart: 18, of which 18 were waited for; matrix products, arithmetic and copies ran while one was open for 0% of the time, Pallas kernels for 0%

profile of v1, /device:TPU:1, one launch (start us, length us, event | category | flops | bytes accessed | tf_op | source)
XLA Modules:
  0.0 991.1 jit_solution(15350385359573245340)
XLA Ops:
  7.2 1.9 copy.36
  9.1 4.5 collective-permute-start
  13.7 5.6 collective-permute-start.1
  19.3 6.1 collective-permute-done
  25.5 0.6 constant_dynamic-update-slice_fusion.1
  26.1 4.0 collective-permute-done.1
  30.3 3.6 collective-permute-start.2
  33.9 1.3 collective-permute-start.3
  35.2 7.6 collective-permute-done.2
  42.8 28.2 %collective-permute-done.3 = f32[32,6,2,512]{3,0,2,1:T(8,128)S(1)} collective-permute-done((f32[32,6,2,512]{3,0,2,1:T(8,128)S(1)}, f32[32,6,2,512]{3,0,2,1:T(8,128)S(1)}, u32[]{:S(2)}, u32[]{:S(2)}) %collective-permute-start.3) | collective-permute-done | bytes 786464 | tf_op jit(solution)/shard_map/ppermute | solution.py:20
  71.0 1.6 broadcast_multiply_fusion
  72.6 2.7 collective-permute-start.4
  75.3 1.9 collective-permute-start.5
  77.3 9.8 collective-permute-done.4
  87.1 4.4 collective-permute-done.5
  91.6 7.8 collective-permute-start.6
  99.4 1.3 collective-permute-start.7
  100.7 7.6 collective-permute-done.6
  108.2 26.3 %collective-permute-done.7 = f32[32,6,2,512]{3,0,2,1:T(8,128)S(1)} collective-permute-done((f32[32,6,2,512]{3,0,2,1:T(8,128)S(1)}, f32[32,6,2,512]{3,0,2,1:T(8,128)S(1)}, u32[]{:S(2)}, u32[]{:S(2)}) %collective-permute-start.7) | collective-permute-done | bytes 786464 | tf_op jit(solution)/shard_map/ppermute | solution.py:20
  134.6 2.4 fusion.21
  136.9 1.9 collective-permute-start.8
  138.9 2.5 collective-permute-start.9
  141.3 9.2 collective-permute-done.8
  150.6 4.4 collective-permute-done.9
  155.1 3.0 collective-permute-start.10
  158.2 1.3 collective-permute-start.11
  159.5 7.5 collective-permute-done.10
  167.0 24.4 %collective-permute-done.11 = f32[32,6,2,512]{3,0,2,1:T(8,128)S(1)} collective-permute-done((f32[32,6,2,512]{3,0,2,1:T(8,128)S(1)}, f32[32,6,2,512]{3,0,2,1:T(8,128)S(1)}, u32[]{:S(2)}, u32[]{:S(2)}) %collective-permute-start.11) | collective-permute-done | bytes 786464 | tf_op jit(solution)/shard_map/ppermute | solution.py:20
  191.4 1.8 fusion.32
  193.2 1.9 collective-permute-start.12
  195.1 2.5 collective-permute-start.13
  197.7 9.1 collective-permute-done.12
  206.8 22.0 %collective-permute-done.13 = f32[32,2,8,512]{3,0,2,1:T(8,128)S(1)} collective-permute-done((f32[32,2,8,512]{3,0,2,1:T(8,128)S(1)}, f32[32,2,8,512]{3,0,2,1:T(8,128)S(1)}, u32[]{:S(2)}, u32[]{:S(2)}) %collective-permute-start.13) | collective-permute-done | bytes 1048608 | tf_op jit(solution)/shard_map/ppermute | solution.py:20
  228.8 1.5 pad_maximum_fusion.30
  230.3 3.5 collective-permute-start.14
  233.7 1.5 collective-permute-start.15
  235.2 0.6 copy.46
  235.9 6.1 collective-permute-done.14
  242.1 27.8 %collective-permute-done.15 = f32[32,6,2,512]{3,0,2,1:T(8,128)} collective-permute-done((f32[32,6,2,512]{3,0,2,1:T(8,128)}, f32[32,6,2,512]{3,0,2,1:T(8,128)}, u32[]{:S(2)}, u32[]{:S(2)}) %collective-permute-start.15) | collective-permute-done | bytes 786464 | tf_op jit(solution)/shard_map/ppermute | solution.py:20
  269.9 3.2 fusion.40
  273.0 1.6 copy.47
  274.6 1.3 concatenate.101
  275.9 2.0 fusion
  277.9 2.1 convolution_bitcast_fusion
  280.0 2.7 copy.57
  282.8 13.0 %gather_fusion = f32[4096,64]{1,0:T(8,128)S(1)} fusion(f32[64,8192]{0,1:T(8,128)} %bitcast.60, s32[4096]{0:T(1024)S(1)} %broadcast_clamp_fusion), kind=kCustom, calls=%fused_computation | custom fusion | bytes 2113536 | tf_op jit(solution)/shard_map/jit(_take)/gather | solution.py:63
  295.7 1.6 copy.49
  297.3 2.3 select_multiply_fusion
  299.6 0.3 all-reduce.9.cloned.1.call-start
  299.9 499.0 %all-reduce.7.cloned.1.call-done = f32[2,32,4096]{2,1,0:T(8,128)} async-done(((f32[2,32,4096]{2,1,0:T(8,128)}), f32[2,32,4096]{2,1,0:T(8,128)}) %all-reduce.7.cloned.1.call-update) | async-done | bytes 1048592 | tf_op jit(solution)/shard_map/psum | solution.py:67
  799.0 0.6 copy.59
  799.6 168.5 %all-reduce.9.cloned.1.call-done = f32[2,32,4096]{2,1,0:T(8,128)} async-done(((f32[2,32,4096]{2,1,0:T(8,128)}), f32[2,32,4096]{2,1,0:T(8,128)}) %all-reduce.9.cloned.1.call-update) | async-done | bytes 1048592 | tf_op jit(solution)/shard_map/psum | solution.py:67
  968.0 1.8 fusion.81
  969.9 2.9 cholesky.17
  972.8 0.6 compare_reduce_fusion
  973.5 0.7 fusion.117
  974.1 2.4 custom-call.6
  976.6 0.2 fusion.120
  976.8 1.8 convolution_multiply_fusion
  979.0 0.6 fusion.119
  979.6 1.6 fusion.78
  981.2 1.6 copy.54
  982.7 0.8 constant_dynamic-slice_fusion
  983.6 0.7 copy.55
  (42 shorter events, 1.3 us)
Async XLA Ops:
  7.2 18.3 %copy-start = (f32[32,2,8,512]{3,2,1,0:T(8,128)S(1)}, f32[32,2,8,512]{3,2,1,0:T(8,128)}, u32[]{:S(2)}) copy-start(f32[32,2,8,512]{3,2,1,0:T(8,128)} %param.4) | copy-start | bytes 3145732
  7.2 791.8 %all-reduce.7.cloned.1.call-start = ((), (), s32[]{:S(2)}) async-start(), calls=%async_computation | async-start | bytes 2097152 | tf_op jit(solution)/shard_map/psum | solution.py:67
  9.1 16.2 %collective-permute-start = (f32[32,2,8,512]{3,0,2,1:T(8,128)S(1)}, f32[32,2,8,512]{3,0,2,1:T(8,128)S(1)}, u32[]{:S(2)}, u32[]{:S(2)}) collective-permute-start(f32[32,2,8,512]{3,0,2,1:T(8,128)S(1)} %copy.36), channel_id=1, source_target_pairs={{0,16},{16,32},{32,48},{48,64},{64,80},{80,96},{96,112},{112,128},... | collective-permute-start | bytes 3145736 | tf_op jit(solution)/shard_map/ppermute | solution.py:19
  13.7 16.4 %collective-permute-start.1 = (f32[32,2,8,512]{3,0,2,1:T(8,128)S(1)}, f32[32,2,8,512]{3,0,2,1:T(8,128)S(1)}, u32[]{:S(2)}, u32[]{:S(2)}) collective-permute-start(f32[32,2,8,512]{3,0,2,1:T(8,128)S(1)} %copy.36), channel_id=1, source_target_pairs={{16,0},{32,16},{48,32},{64,48},{80,64},{96,80},{112,96},{128,112},... | collective-permute-start | bytes 3145736 | tf_op jit(solution)/shard_map/ppermute | solution.py:20
  30.2 40.8 %copy-start.3 = (f32[2,8,512]{2,1,0:T(8,128)S(1)}, f32[2,8,512]{2,1,0:T(8,128)}, u32[]{:S(2)}) copy-start(f32[2,8,512]{2,1,0:T(8,128)} %param.5) | copy-start | bytes 98308
  30.3 12.5 %collective-permute-start.2 = (f32[32,6,2,512]{3,0,2,1:T(8,128)S(1)}, f32[32,6,2,512]{3,0,2,1:T(8,128)S(1)}, u32[]{:S(2)}, u32[]{:S(2)}) collective-permute-start(f32[32,6,2,512]{3,0,2,1:T(8,128)S(1)} %get-tuple-element.23), channel_id=1, source_target_pairs={{0,1},{1,2},{2,3},{3,4},{4,5},{5,6},{6,7},{7,8},{8,9},{9,10},{10,1... | collective-permute-start | bytes 2359304 | tf_op jit(solution)/shard_map/ppermute | solution.py:19
  33.9 37.1 %collective-permute-start.3 = (f32[32,6,2,512]{3,0,2,1:T(8,128)S(1)}, f32[32,6,2,512]{3,0,2,1:T(8,128)S(1)}, u32[]{:S(2)}, u32[]{:S(2)}) collective-permute-start(f32[32,6,2,512]{3,0,2,1:T(8,128)S(1)} %get-tuple-element.24), channel_id=1, source_target_pairs={{1,0},{2,1},{3,2},{4,3},{5,4},{6,5},{7,6},{8,7},{9,8},{10,9},{11,1... | collective-permute-start | bytes 2359304 | tf_op jit(solution)/shard_map/ppermute | solution.py:20
  72.6 14.4 %collective-permute-start.4 = (f32[32,2,8,512]{3,0,2,1:T(8,128)S(1)}, f32[32,2,8,512]{3,0,2,1:T(8,128)S(1)}, u32[]{:S(2)}, u32[]{:S(2)}) collective-permute-start(f32[32,2,8,512]{3,0,2,1:T(8,128)S(1)} %get-tuple-element.15), channel_id=1, source_target_pairs={{0,16},{16,32},{32,48},{48,64},{64,80},{80,96},{96,112},{112,128},... | collective-permute-start | bytes 3145736 | tf_op jit(solution)/shard_map/ppermute | solution.py:19
  75.3 16.1 %collective-permute-start.5 = (f32[32,2,8,512]{3,0,2,1:T(8,128)S(1)}, f32[32,2,8,512]{3,0,2,1:T(8,128)S(1)}, u32[]{:S(2)}, u32[]{:S(2)}) collective-permute-start(f32[32,2,8,512]{3,0,2,1:T(8,128)S(1)} %get-tuple-element.15), channel_id=1, source_target_pairs={{16,0},{32,16},{48,32},{64,48},{80,64},{96,80},{112,96},{128,112},... | collective-permute-start | bytes 3145736 | tf_op jit(solution)/shard_map/ppermute | solution.py:20
  91.6 16.7 %collective-permute-start.6 = (f32[32,6,2,512]{3,0,2,1:T(8,128)S(1)}, f32[32,6,2,512]{3,0,2,1:T(8,128)S(1)}, u32[]{:S(2)}, u32[]{:S(2)}) collective-permute-start(f32[32,6,2,512]{3,0,2,1:T(8,128)S(1)} %get-tuple-element.21), channel_id=1, source_target_pairs={{0,1},{1,2},{2,3},{3,4},{4,5},{5,6},{6,7},{7,8},{8,9},{9,10},{10,1... | collective-permute-start | bytes 2359304 | tf_op jit(solution)/shard_map/ppermute | solution.py:19
  99.4 35.2 %collective-permute-start.7 = (f32[32,6,2,512]{3,0,2,1:T(8,128)S(1)}, f32[32,6,2,512]{3,0,2,1:T(8,128)S(1)}, u32[]{:S(2)}, u32[]{:S(2)}) collective-permute-start(f32[32,6,2,512]{3,0,2,1:T(8,128)S(1)} %get-tuple-element.22), channel_id=1, source_target_pairs={{1,0},{2,1},{3,2},{4,3},{5,4},{6,5},{7,6},{8,7},{9,8},{10,9},{11,1... | collective-permute-start | bytes 2359304 | tf_op jit(solution)/shard_map/ppermute | solution.py:20
  136.9 13.7 %collective-permute-start.8 = (f32[32,2,8,512]{3,0,2,1:T(8,128)S(1)}, f32[32,2,8,512]{3,0,2,1:T(8,128)S(1)}, u32[]{:S(2)}, u32[]{:S(2)}) collective-permute-start(f32[32,2,8,512]{3,0,2,1:T(8,128)S(1)} %fusion.21), channel_id=1, source_target_pairs={{0,16},{16,32},{32,48},{48,64},{64,80},{80,96},{96,112},{112,128},... | collective-permute-start | bytes 3145736 | tf_op jit(solution)/shard_map/ppermute | solution.py:19
  138.9 16.1 %collective-permute-start.9 = (f32[32,2,8,512]{3,0,2,1:T(8,128)S(1)}, f32[32,2,8,512]{3,0,2,1:T(8,128)S(1)}, u32[]{:S(2)}, u32[]{:S(2)}) collective-permute-start(f32[32,2,8,512]{3,0,2,1:T(8,128)S(1)} %fusion.21), channel_id=1, source_target_pairs={{16,0},{32,16},{48,32},{64,48},{80,64},{96,80},{112,96},{128,112},... | collective-permute-start | bytes 3145736 | tf_op jit(solution)/shard_map/ppermute | solution.py:20
  155.1 11.9 %collective-permute-start.10 = (f32[32,6,2,512]{3,0,2,1:T(8,128)S(1)}, f32[32,6,2,512]{3,0,2,1:T(8,128)S(1)}, u32[]{:S(2)}, u32[]{:S(2)}) collective-permute-start(f32[32,6,2,512]{3,0,2,1:T(8,128)S(1)} %get-tuple-element.19), channel_id=1, source_target_pairs={{0,1},{1,2},{2,3},{3,4},{4,5},{5,6},{6,7},{7,8},{8,9},{9,10},{10,1... | collective-permute-start | bytes 2359304 | tf_op jit(solution)/shard_map/ppermute | solution.py:19
  158.1 39.4 %copy-start.5 = (s32[2,8,512]{2,1,0:T(8,128)S(1)}, s32[2,8,512]{2,1,0:T(8,128)}, u32[]{:S(2)}) copy-start(s32[2,8,512]{2,1,0:T(8,128)} %param.6) | copy-start | bytes 98308
  158.2 39.5 %slice-start = ((s32[1,1,8192]{2,1,0:T(1,128)}), s32[1,1,4096]{2,1,0:T(1,128)S(1)}, s32[]{:S(2)}) async-start(s32[1,1,8192]{2,1,0:T(1,128)} %param.7), calls=%async_computation.2 | async-start | bytes 32768 | tf_op jit(solution)/shard_map/slice | solution.py:63
  158.2 33.2 %collective-permute-start.11 = (f32[32,6,2,512]{3,0,2,1:T(8,128)S(1)}, f32[32,6,2,512]{3,0,2,1:T(8,128)S(1)}, u32[]{:S(2)}, u32[]{:S(2)}) collective-permute-start(f32[32,6,2,512]{3,0,2,1:T(8,128)S(1)} %get-tuple-element.20), channel_id=1, source_target_pairs={{1,0},{2,1},{3,2},{4,3},{5,4},{6,5},{7,6},{8,7},{9,8},{10,9},{11,1... | collective-permute-start | bytes 2359304 | tf_op jit(solution)/shard_map/ppermute | solution.py:20
  193.2 13.7 %collective-permute-start.12 = (f32[32,2,8,512]{3,0,2,1:T(8,128)S(1)}, f32[32,2,8,512]{3,0,2,1:T(8,128)S(1)}, u32[]{:S(2)}, u32[]{:S(2)}) collective-permute-start(f32[32,2,8,512]{3,0,2,1:T(8,128)S(1)} %fusion.32), channel_id=1, source_target_pairs={{0,16},{16,32},{32,48},{48,64},{64,80},{80,96},{96,112},{112,128},... | collective-permute-start | bytes 3145736 | tf_op jit(solution)/shard_map/ppermute | solution.py:19
  195.1 33.7 %collective-permute-start.13 = (f32[32,2,8,512]{3,0,2,1:T(8,128)S(1)}, f32[32,2,8,512]{3,0,2,1:T(8,128)S(1)}, u32[]{:S(2)}, u32[]{:S(2)}) collective-permute-start(f32[32,2,8,512]{3,0,2,1:T(8,128)S(1)} %fusion.32), channel_id=1, source_target_pairs={{16,0},{32,16},{48,32},{64,48},{80,64},{96,80},{112,96},{128,112},... | collective-permute-start | bytes 3145736 | tf_op jit(solution)/shard_map/ppermute | solution.py:20
  197.7 37.5 %copy-start.4 = (s32[1,1,8192]{2,1,0:T(1,128)S(1)}, s32[1,1,8192]{2,1,0:T(1,128)}, u32[]{:S(2)}) copy-start(s32[1,1,8192]{2,1,0:T(1,128)} %param.7) | copy-start | bytes 98308
  206.8 23.4 %copy-start.1 = (f32[32,2,8,512]{3,0,2,1:T(8,128)}, f32[32,2,8,512]{3,0,2,1:T(8,128)S(1)}, u32[]{:S(2)}) copy-start(f32[32,2,8,512]{3,0,2,1:T(8,128)S(1)} %collective-permute-done.12) | copy-start | bytes 3145732
  228.8 1.5 copy-start.2
  230.3 11.8 %collective-permute-start.14 = (f32[32,6,2,512]{3,0,2,1:T(8,128)}, f32[32,6,2,512]{3,0,2,1:T(8,128)}, u32[]{:S(2)}, u32[]{:S(2)}) collective-permute-start(f32[32,6,2,512]{3,0,2,1:T(8,128)} %get-tuple-element.17), channel_id=1, source_target_pairs={{0,1},{1,2},{2,3},{3,4},{4,5},{5,6},{6,7},{7,8},{8,9},{9,10},{10,1... | collective-permute-start | bytes 2359304 | tf_op jit(solution)/shard_map/ppermute | solution.py:19
  233.7 36.1 %collective-permute-start.15 = (f32[32,6,2,512]{3,0,2,1:T(8,128)}, f32[32,6,2,512]{3,0,2,1:T(8,128)}, u32[]{:S(2)}, u32[]{:S(2)}) collective-permute-start(f32[32,6,2,512]{3,0,2,1:T(8,128)} %get-tuple-element.18), channel_id=1, source_target_pairs={{1,0},{2,1},{3,2},{4,3},{5,4},{6,5},{7,6},{8,7},{9,8},{10,9},{11,1... | collective-permute-start | bytes 2359304 | tf_op jit(solution)/shard_map/ppermute | solution.py:20
  299.6 668.4 %all-reduce.9.cloned.1.call-start = ((), (), s32[]{:S(2)}) async-start(), calls=%async_computation.1 | async-start | bytes 2097152 | tf_op jit(solution)/shard_map/psum | solution.py:67
Sparse Core Ops, SparseCore 0:
  299.7 499.1 all-reduce.6
  802.1 165.8 all-reduce.8
